TPU v7x, 512 devices: a whole 4x8x8 slice. The times are simulated.
512 devices in a mesh: segment: 4 (over z_lo), seq: 16 (over z_hi, x, core), mp: 8 (over y).
Axes of the slice: x: 4, y: 8, z: 8 (z_hi: 2, z_lo: 4; z = z_hi * 4 + z_lo), core: 2. Of those that a mesh axis runs over, the one named last changes fastest.
Arguments:
- latents: bfloat16 [4, 16, 256, 4096], P('segment', 'seq', None, 'mp'), may hold values from -6 to 6
- w_qkv: bfloat16 [4, 4096, 3, 4096], P('segment', 'seq', None, 'mp'), may hold values from -1 to 1
- w_out: bfloat16 [4, 4096, 4096], P('segment', 'mp', 'seq'), may hold values from -0.09375 to 0.09375
- mod_shift: float32 [4, 4096], P('segment'), may hold values from -3 to 3
- mod_scale: float32 [4, 4096], P('segment'), may hold values from 0.1 to 1.9
- mod_gate: float32 [4, 4096], P('segment'), may hold values from 0.5 to 1.5
- counts: int32 [4, 16], P('segment'), may hold values from 64 to 256, as said below
Outputs:
- next_latents: bfloat16 [4, 16, 256, 4096], P('segment', 'seq', None, 'mp')
Inputs may be any that keep to these rules, and one draw needn't show every extreme that they name: `counts`: in every section's clip at least one frame has all 256 patch positions valid.
All inputs are finite; a program needn't handle non-finite values.
Results may differ from a plain program's by a relative error of at most 0.01.
Values may be sent and summed in bfloat16 or wider, within the bound.
No kernel may reach another device: no remote copies, remote signals or barrier semaphores. Data moves between devices by JAX's collectives and lax.ppermute only.
A program may use at most 64 MiB of HBM per device.

v0:
```python
import math

import jax
import jax.numpy as jnp
from jax import lax
from jax.sharding import PartitionSpec as P


HD = 128


EPS = 1e-06
NEG_FILL = -1e30


def masked_attention(queries, keys_in, values, usable):
    factor = 1.0 / math.sqrt(queries.shape[-1])
    scores = (
        jnp.einsum("...ihe,...jhe->...hij", queries, keys_in, preferred_element_type=jnp.float32)
        * factor
    )
    allowed = usable[..., None, :, None] & usable[..., None, None, :]
    masked = jnp.where(allowed, scores, NEG_FILL)
    highest = jnp.max(masked, axis=-1, keepdims=True)
    raised = jnp.where(allowed, jnp.exp(masked - highest), 0.0)
    spare_one = jnp.where(usable, 0.0, 1.0)[..., None, :, None]
    weights = (raised / (jnp.sum(raised, axis=-1, keepdims=True) + spare_one)).astype(jnp.bfloat16)
    blended = jnp.einsum(
        "...hij,...jhe->...ihe", weights, values, preferred_element_type=jnp.float32
    )
    return blended.astype(jnp.bfloat16)


SEQ = ("zh", "x", "c")


def seq_index():
    return (lax.axis_index("zh") * lax.axis_size("x") + lax.axis_index("x")) * lax.axis_size(
        "c"
    ) + lax.axis_index("c")


def swap(block, axis):
    return lax.ppermute(block, axis, [(0, 1), (1, 0)])


def spread_seq(block):
    zh = lax.axis_index("zh")
    x = lax.axis_index("x")
    c = lax.axis_index("c")
    nx = lax.axis_size("x")
    held = [(zh, x, block), (1 - zh, x, swap(block, "zh"))]
    reached = []
    for bz, bx, piece in held:
        reached.append((bz, bx, piece))
        if nx == 4:
            ahead = lax.ppermute(piece, "x", [(k, (k + 1) % nx) for k in range(nx)])
            behind = lax.ppermute(piece, "x", [(k, (k - 1) % nx) for k in range(nx)])
            onward = jnp.where(c == 0, ahead, behind)
            pairs = [(k * 2, ((k + 1) % nx) * 2) for k in range(nx)]
            pairs += [(k * 2 + 1, ((k - 1) % nx) * 2 + 1) for k in range(nx)]
            far = lax.ppermute(onward, ("x", "c"), pairs)
            reached.append((bz, (bx - 1) % nx, ahead))
            reached.append((bz, (bx + 1) % nx, behind))
            reached.append((bz, (bx + 2) % nx, far))
        else:
            for s in range(1, nx):
                moved = lax.ppermute(piece, "x", [(k, (k + s) % nx) for k in range(nx)])
                reached.append((bz, (bx - s) % nx, moved))
    return [(bz * nx + bx, piece) for bz, bx, piece in reached]


def relay_onward(rows_now):
    halves = lax.axis_size("zh")
    sections = lax.axis_size("segment")
    zh = lax.axis_index("zh")
    split = rows_now.reshape((halves, -1) + rows_now.shape[1:])
    local = lax.all_to_all(split, ("x", "c"), split_axis=1, concat_axis=1, tiled=True)
    stay = jnp.where(zh == 0, local[0], local[1])
    cross = jnp.where(zh == 0, local[1], local[0])
    to = lambda s, h: s * halves + h
    stay = lax.ppermute(
        stay,
        ("segment", "zh"),
        [(to(s, h), to((s + 1) % sections, h)) for s in range(sections) for h in range(halves)],
    )
    cross = lax.ppermute(
        cross,
        ("segment", "zh"),
        [(to(s, h), to((s + 1) % sections, 1 - h)) for s in range(sections) for h in range(halves)],
    )
    return jnp.where(
        zh == 0, jnp.concatenate([stay, cross], axis=0), jnp.concatenate([cross, stay], axis=0)
    )


def on_device(latents, w_qkv, w_out, mod_shift, mod_scale, mod_gate, counts):
    frames = lax.axis_size(SEQ)
    patches = latents.shape[2]
    narrow = latents.shape[3]
    span = patches // frames
    segment_rows = latents[0, 0]
    gathered = lax.all_gather(latents, "mp", axis=3, tiled=True)[0, 0]
    widened = gathered.astype(jnp.float32)
    average = jnp.mean(widened, axis=-1, keepdims=True)
    centred = widened - average
    variance = jnp.mean(centred * centred, axis=-1, keepdims=True)
    modulated = (centred * lax.rsqrt(variance + EPS) * mod_scale[0] + mod_shift[0]).astype(
        jnp.bfloat16
    )
    columns = w_qkv.shape[2] * w_qkv.shape[3]
    rows = w_qkv.shape[1]
    payload = jnp.concatenate([w_qkv[0].reshape(rows, columns), w_out[0].T], axis=1)
    arrived = spread_seq(payload)
    core = lax.axis_index("c")
    pair_rows = jnp.concatenate([modulated, swap(modulated, "c")], axis=0)
    w_in = jnp.concatenate([piece[:, :columns] for _, piece in arrived], axis=0)
    reordered = jnp.concatenate(
        [
            lax.dynamic_slice_in_dim(pair_rows, (chip * 2 + core) * rows, rows, axis=1)
            for chip, _ in arrived
        ],
        axis=1,
    )
    both = jnp.dot(reordered, w_in, preferred_element_type=jnp.float32)
    projected = both[:patches] + swap(both[patches:].astype(jnp.bfloat16), "c").astype(
        jnp.float32
    )
    local_heads = w_qkv.shape[3] // HD
    projected = projected.astype(jnp.bfloat16).reshape(patches, 3, local_heads, HD)
    frame_here = seq_index()
    clip_counts = counts[0]
    positions = jnp.arange(frames)

    def spatial(triple):
        count_here = jnp.sum(jnp.where(positions == frame_here, clip_counts, 0))
        usable = jnp.arange(patches) < count_here
        return masked_attention(triple[:, 0], triple[:, 1], triple[:, 2], usable)

    def temporal(triple):
        by_place = triple.reshape(frames, span, 3, local_heads, HD).transpose(1, 0, 2, 3, 4)
        location = frame_here * span + jnp.arange(span)
        usable = location[:, None] < clip_counts[None, :]
        blended = masked_attention(by_place[:, :, 0], by_place[:, :, 1], by_place[:, :, 2], usable)
        return blended.transpose(1, 0, 2, 3).reshape(patches, local_heads, HD)

    attended = lax.cond(lax.axis_index("segment") % 2 == 0, spatial, temporal, projected)
    attended = attended.reshape(patches, local_heads * HD)
    member = lax.axis_index("mp")
    width = w_out.shape[2]
    pair_att = jnp.concatenate([attended, swap(attended, "c")], axis=0)
    w_back = jnp.concatenate([piece[:, columns:] for _, piece in arrived], axis=0)
    mixed = jnp.einsum(
        "tr,cr->tc", pair_att, w_back, preferred_element_type=jnp.float32
    ).astype(jnp.bfloat16)
    partials = jnp.zeros((2 * patches, width * frames // 2), jnp.bfloat16)
    for slot, (chip, _) in enumerate(arrived):
        partials = lax.dynamic_update_slice_in_dim(
            partials, mixed[:, slot * width : (slot + 1) * width], chip * width, axis=1
        )
    pair_sum = lax.psum_scatter(partials, "mp", scatter_dimension=1, tiled=True)
    mine = pair_sum[:patches]
    theirs = swap(pair_sum[patches:], "c")
    summed = jnp.where(
        core == 0,
        jnp.concatenate([mine, theirs], axis=1),
        jnp.concatenate([theirs, mine], axis=1),
    ).astype(jnp.float32)
    gate_here = lax.dynamic_slice_in_dim(mod_gate[0], member * narrow, narrow)
    updated = (segment_rows.astype(jnp.float32) + gate_here * summed).astype(jnp.bfloat16)
    updated = updated.reshape(frames, span, narrow)
    moved = relay_onward(updated)
    return moved.reshape(1, 1, patches, narrow)


def solution(mesh):
    seg, seq, mp = mesh.devices.shape
    inner = mesh.devices.reshape(seg, 2, seq // 4, 2, mp)
    fine = jax.sharding.Mesh(inner, ("segment", "zh", "x", "c", "mp"))
    return jax.shard_map(
        on_device,
        mesh=fine,
        in_specs=(
            P("segment", SEQ, None, "mp"),
            P("segment", SEQ, None, "mp"),
            P("segment", "mp", SEQ),
            P("segment", None),
            P("segment", None),
            P("segment", None),
            P("segment", None),
        ),
        out_specs=P("segment", SEQ, None, "mp"),
        check_vma=False,
    )
```

profile of v0, /device:TPU:1, one launch (start us, length us, event | category | flops | bytes accessed | tf_op | source)
XLA Modules:
  0.0 238.6 jit_solution(18230542133836770403)
XLA Ops:
  7.3 1.4 copy.41
  8.7 2.0 pad_maximum_fusion
  10.7 3.9 %collective-permute-start.1 = (bf16[256,2048]{0,1:T(8,128)(2,1)}, bf16[256,2048]{0,1:T(8,128)(2,1)S(1)}, u32[]{:S(2)}, u32[]{:S(2)}) collective-permute-start(bf16[256,2048]{0,1:T(8,128)(2,1)} %pad_maximum_fusion), channel_id=1, source_target_pairs={{0,16},{16,32},{32,48},{48,0},{1,17},{17,33},{33,49},{49,1},{2,18}... | collective-permute-start | bytes 3145736 | tf_op jit(solution)/shard_map/ppermute | solution.py:57
  14.7 3.2 %collective-permute-start.2 = (bf16[256,2048]{0,1:T(8,128)(2,1)}, bf16[256,2048]{0,1:T(8,128)(2,1)S(1)}, u32[]{:S(2)}, u32[]{:S(2)}) collective-permute-start(bf16[256,2048]{0,1:T(8,128)(2,1)} %pad_maximum_fusion), channel_id=1, source_target_pairs={{0,48},{16,0},{32,16},{48,32},{1,49},{17,1},{33,17},{49,33},{2,50}... | collective-permute-start | bytes 3145736 | tf_op jit(solution)/shard_map/ppermute | solution.py:58
  17.9 10.8 %collective-permute-start.4 = (bf16[256,2048]{0,1:T(8,128)(2,1)}, bf16[256,2048]{0,1:T(8,128)(2,1)}, u32[]{:S(2)}, u32[]{:S(2)}) collective-permute-start(bf16[256,2048]{0,1:T(8,128)(2,1)} %pad_maximum_fusion), channel_id=1, source_target_pairs={{0,64},{64,0},{1,65},{65,1},{2,66},{66,2},{3,67},{67,3},{4,68},{68... | collective-permute-start | bytes 3145736 | tf_op jit(solution)/shard_map/ppermute | solution.py:44
  28.8 0.7 constant_dynamic-update-slice_fusion.1
  29.7 3.6 %collective-permute-done.1 = bf16[256,2048]{0,1:T(8,128)(2,1)S(1)} collective-permute-done((bf16[256,2048]{0,1:T(8,128)(2,1)}, bf16[256,2048]{0,1:T(8,128)(2,1)S(1)}, u32[]{:S(2)}, u32[]{:S(2)}) %collective-permute-start.1) | collective-permute-done | bytes 1048608 | tf_op jit(solution)/shard_map/ppermute | solution.py:57
  33.3 3.5 %collective-permute-done.2 = bf16[256,2048]{0,1:T(8,128)(2,1)S(1)} collective-permute-done((bf16[256,2048]{0,1:T(8,128)(2,1)}, bf16[256,2048]{0,1:T(8,128)(2,1)S(1)}, u32[]{:S(2)}, u32[]{:S(2)}) %collective-permute-start.2) | collective-permute-done | bytes 1048608 | tf_op jit(solution)/shard_map/ppermute | solution.py:58
  36.8 1.1 broadcast_select_fusion.3
  37.9 5.4 %collective-permute-start.3 = (bf16[256,2048]{0,1:T(8,128)(2,1)}, bf16[256,2048]{0,1:T(8,128)(2,1)}, u32[]{:S(2)}, u32[]{:S(2)}) collective-permute-start(bf16[256,2048]{0,1:T(8,128)(2,1)} %broadcast_select_fusion.3), channel_id=1, source_target_pairs={{0,16},{16,32},{32,48},{48,0},{8,56},{24,8},{40,24},{56,40},{1,17}... | collective-permute-start | bytes 3145736 | tf_op jit(solution)/shard_map/ppermute | solution.py:62
  43.3 7.3 %collective-permute-done.4 = bf16[256,2048]{0,1:T(8,128)(2,1)} collective-permute-done((bf16[256,2048]{0,1:T(8,128)(2,1)}, bf16[256,2048]{0,1:T(8,128)(2,1)}, u32[]{:S(2)}, u32[]{:S(2)}) %collective-permute-start.4) | collective-permute-done | bytes 1048608 | tf_op jit(solution)/shard_map/ppermute | solution.py:44
  50.5 2.0 collective-permute-start.5
  52.6 4.4 %collective-permute-start.6 = (bf16[256,2048]{0,1:T(8,128)(2,1)}, bf16[256,2048]{0,1:T(8,128)(2,1)S(1)}, u32[]{:S(2)}, u32[]{:S(2)}) collective-permute-start(bf16[256,2048]{0,1:T(8,128)(2,1)} %collective-permute-done.4), channel_id=1, source_target_pairs={{0,48},{16,0},{32,16},{48,32},{1,49},{17,1},{33,17},{49,33},{2,50}... | collective-permute-start | bytes 3145736 | tf_op jit(solution)/shard_map/ppermute | solution.py:58
  57.0 0.8 slice_dynamic-update-slice_fusion.21
  58.0 21.0 %collective-permute-done.5 = bf16[256,2048]{0,1:T(8,128)(2,1)S(1)} collective-permute-done((bf16[256,2048]{0,1:T(8,128)(2,1)}, bf16[256,2048]{0,1:T(8,128)(2,1)S(1)}, u32[]{:S(2)}, u32[]{:S(2)}) %collective-permute-start.5) | collective-permute-done | bytes 1048608 | tf_op jit(solution)/shard_map/ppermute | solution.py:57
  79.0 1.0 copy-done.3
  80.0 1.1 broadcast_select_fusion.2
  81.1 2.9 %collective-permute-start.7 = (bf16[256,2048]{0,1:T(8,128)(2,1)}, bf16[256,2048]{0,1:T(8,128)(2,1)}, u32[]{:S(2)}, u32[]{:S(2)}) collective-permute-start(bf16[256,2048]{0,1:T(8,128)(2,1)} %broadcast_select_fusion.2), channel_id=1, source_target_pairs={{0,16},{16,32},{32,48},{48,0},{8,56},{24,8},{40,24},{56,40},{1,17}... | collective-permute-start | bytes 3145736 | tf_op jit(solution)/shard_map/ppermute | solution.py:62
  84.1 2.1 convert_reduce_fusion
  87.0 1.0 fusion.30
  88.1 6.3 %collective-permute-start = (bf16[256,4096]{1,0:T(8,128)(2,1)S(1)}, bf16[256,4096]{1,0:T(8,128)(2,1)S(1)}, u32[]{:S(2)}, u32[]{:S(2)}) collective-permute-start(bf16[256,4096]{1,0:T(8,128)(2,1)S(1)} %fusion.30), channel_id=1, source_target_pairs={{0,8},{8,0},{1,9},{9,1},{2,10},{10,2},{3,11},{11,3},{4,12},{12,4},... | collective-permute-start | bytes 6291464 | tf_op jit(solution)/shard_map/ppermute | solution.py:44
  94.4 1.2 slice_dynamic-update-slice_fusion.4
  95.6 1.2 slice_dynamic-update-slice_fusion.3
  97.3 1.2 slice_dynamic-update-slice_fusion
  99.0 3.5 %fusion.58 = f32[512,1536]{1,0:T(8,128)S(1)} fusion(bf16[512,2048]{1,0:T(8,128)(2,1)S(1)} %fusion.37, bf16[2048,1536]{0,1:T(8,128)(2,1)S(1)} %slice_dynamic-update-slice_fusion), kind=kOutput, calls=%fused_computation.136 | convolution fusion | flops 3221225472 | bytes 11534336 | tf_op jit(solution)/shard_map/dot_general | solution.py:125
  102.5 9.0 %collective-permute-start.8 = (bf16[256,1536]{1,0:T(8,128)(2,1)S(1)}, bf16[256,1536]{1,0:T(8,128)(2,1)S(1)}, u32[]{:S(2)}, u32[]{:S(2)}) collective-permute-start(bf16[256,1536]{1,0:T(8,128)(2,1)S(1)} %slice.225), channel_id=1, source_target_pairs={{0,8},{8,0},{1,9},{9,1},{2,10},{10,2},{3,11},{11,3},{4,12},{12,4},... | collective-permute-start | bytes 2359304 | tf_op jit(solution)/shard_map/ppermute | solution.py:44
  111.5 0.8 slice_dynamic-update-slice_fusion.20
  112.2 1.7 slice_dynamic-update-slice_fusion.19
  114.0 1.7 slice_dynamic-update-slice_fusion.18
  115.7 0.8 slice_dynamic-update-slice_fusion.17
  116.7 3.8 %conditional.1 = (bf16[256,512]{0,1:T(8,128)(2,1)S(1)}) conditional(s32[]{:T(128)} %convert_element_type.58, (s32[]{:T(128)}, s32[1,16]{1,0:T(1,128)S(1)}, bf16[256,1536]{1,0:T(8,128)(2,1)S(1)}) %tuple.25, (s32[]{:T(128)}, s32[16]{0:T(128)S(1)}, s32[1,16]{1,0:T(1,128)S(1)}, bf16[256,1536]{1,0:T(8,128)(2,1)S(1)}) %tuple.26), branch_computations={%region_2.5_spmd, %region_5.9_spmd} | conditional | flops 204410160 | bytes 6552408 | solution.py:147
  119.7 0.8 convolution_convert_fusion.1
  120.5 1.9 collective-permute-start.9
  122.4 0.8 slice_dynamic-update-slice_fusion.16
  123.2 1.7 slice_dynamic-update-slice_fusion.15
  124.9 2.9 %convolution_convert_fusion.2 = bf16[512,2048]{1,0:T(8,128)(2,1)S(1)} fusion(bf16[2048,512]{0,1:T(8,128)(2,1)} %slice_dynamic-update-slice_fusion.15, bf16[256,512]{0,1:T(8,128)(2,1)S(1)} %collective-permute-done.9, bf16[256,512]{0,1:T(8,128)(2,1)S(1)} %get-tuple-element.46), kind=kOutput, calls=%fused_computation.71 | convolution fusion | flops 1075838976 | bytes 4718592 | tf_op jit(solution)/shard_map/tr,cr->tc/dot_general | solution.py:153
  128.5 1.3 copy-done.2
  129.8 62.2 %reduce-scatter.2.cloned.1.call-done = bf16[512,256]{1,0:T(8,128)(2,1)} async-done(((bf16[512,2048]{1,0:T(8,128)(2,1)}), bf16[512,256]{1,0:T(8,128)(2,1)}) %reduce-scatter.2.cloned.1.call-update) | async-done | bytes 262160 | tf_op jit(solution)/shard_map/reduce_scatter | solution.py:161
  192.0 1.0 fusion.57
  193.0 7.2 %collective-permute-start.10 = (bf16[256,256]{1,0:T(8,128)(2,1)S(1)}, bf16[256,256]{1,0:T(8,128)(2,1)S(1)}, u32[]{:S(2)}, u32[]{:S(2)}) collective-permute-start(bf16[256,256]{1,0:T(8,128)(2,1)S(1)} %get-tuple-element.45), channel_id=1, source_target_pairs={{0,8},{8,0},{1,9},{9,1},{2,10},{10,2},{3,11},{11,3},{4,12},{12,4},... | collective-permute-start | bytes 393224 | tf_op jit(solution)/shard_map/ppermute | solution.py:44
  200.2 0.9 collective-permute-done.10
  201.2 0.7 copy.43
  202.0 4.6 %all-to-all-start = ((bf16[2,8,16,512]{3,2,0,1:T(8,128)(2,1)}), bf16[2,8,16,512]{3,2,0,1:T(8,128)(2,1)S(1)}, u32[]{:S(2)}, u32[]{:S(2)}) async-start(bf16[2,8,16,512]{3,2,0,1:T(8,128)(2,1)} %copy.43), calls=%async_computation.1 | async-start | bytes 524288 | tf_op jit(solution)/shard_map/all_to_all | solution.py:78
  206.6 6.5 %all-to-all-done = bf16[2,8,16,512]{3,2,0,1:T(8,128)(2,1)S(1)} async-done(((bf16[2,8,16,512]{3,2,0,1:T(8,128)(2,1)}), bf16[2,8,16,512]{3,2,0,1:T(8,128)(2,1)S(1)}, u32[]{:S(2)}, u32[]{:S(2)}) %all-to-all-start) | async-done | bytes 262176 | tf_op jit(solution)/shard_map/all_to_all | solution.py:78
  213.0 3.3 %collective-permute-start.11 = (bf16[8,16,512]{2,1,0:T(8,128)(2,1)S(1)}, bf16[8,16,512]{2,1,0:T(8,128)(2,1)S(1)}, u32[]{:S(2)}, u32[]{:S(2)}) collective-permute-start(bf16[8,16,512]{2,1,0:T(8,128)(2,1)S(1)} %fusion.53), channel_id=1, source_target_pairs={{0,128},{64,192},{128,256},{192,320},{256,384},{320,448},{384,0},{... | collective-permute-start | bytes 393224 | tf_op jit(solution)/shard_map/ppermute | solution.py:82
  216.4 6.1 %collective-permute-start.12 = (bf16[8,16,512]{2,1,0:T(8,128)(2,1)S(1)}, bf16[8,16,512]{2,1,0:T(8,128)(2,1)S(1)}, u32[]{:S(2)}, u32[]{:S(2)}) collective-permute-start(bf16[8,16,512]{2,1,0:T(8,128)(2,1)S(1)} %fusion.52), channel_id=1, source_target_pairs={{0,192},{64,128},{128,320},{192,256},{256,448},{320,384},{384,64},... | collective-permute-start | bytes 393224 | tf_op jit(solution)/shard_map/ppermute | solution.py:87
  222.6 8.5 %collective-permute-done.12 = bf16[8,16,512]{2,1,0:T(8,128)(2,1)S(1)} collective-permute-done((bf16[8,16,512]{2,1,0:T(8,128)(2,1)S(1)}, bf16[8,16,512]{2,1,0:T(8,128)(2,1)S(1)}, u32[]{:S(2)}, u32[]{:S(2)}) %collective-permute-start.12) | collective-permute-done | bytes 131104 | tf_op jit(solution)/shard_map/ppermute | solution.py:87
  231.1 0.7 maximum_select_fusion.1
  (77 shorter events, 6.5 us)
Async XLA Ops:
  6.5 193.6 %copy-start = (f32[1,4096]{1,0:T(1,128)S(1)}, f32[1,4096]{1,0:T(1,128)}, u32[]{:S(2)}) copy-start(f32[1,4096]{1,0:T(1,128)} %param.14) | copy-start | bytes 49156
  6.5 22.3 %copy-start.8 = (bf16[1,512,256]{2,1,0:T(8,128)(2,1)S(1)}, bf16[1,512,256]{2,1,0:T(8,128)(2,1)}, u32[]{:S(2)}) copy-start(bf16[1,512,256]{2,1,0:T(8,128)(2,1)} %param.11) | copy-start | bytes 786436
  6.5 77.5 %all-gather.2.cloned.1.call-start = ((), (), s32[]{:S(2)}) async-start(), calls=%async_computation.2 | async-start | bytes 2359296 | tf_op jit(solution)/shard_map/all_gather | solution.py:103
  7.3 184.7 %reduce-scatter.2.cloned.1.call-start = ((), (), s32[]{:S(2)}) async-start(), calls=%async_computation.3 | async-start | bytes 2359296 | tf_op jit(solution)/shard_map/reduce_scatter | solution.py:161
  10.7 22.5 %collective-permute-start.1 = (bf16[256,2048]{0,1:T(8,128)(2,1)}, bf16[256,2048]{0,1:T(8,128)(2,1)S(1)}, u32[]{:S(2)}, u32[]{:S(2)}) collective-permute-start(bf16[256,2048]{0,1:T(8,128)(2,1)} %pad_maximum_fusion), channel_id=1, source_target_pairs={{0,16},{16,32},{32,48},{48,0},{1,17},{17,33},{33,49},{49,1},{2,18}... | collective-permute-start | bytes 3145736 | tf_op jit(solution)/shard_map/ppermute | solution.py:57
  14.7 22.1 %collective-permute-start.2 = (bf16[256,2048]{0,1:T(8,128)(2,1)}, bf16[256,2048]{0,1:T(8,128)(2,1)S(1)}, u32[]{:S(2)}, u32[]{:S(2)}) collective-permute-start(bf16[256,2048]{0,1:T(8,128)(2,1)} %pad_maximum_fusion), channel_id=1, source_target_pairs={{0,48},{16,0},{32,16},{48,32},{1,49},{17,1},{33,17},{49,33},{2,50}... | collective-permute-start | bytes 3145736 | tf_op jit(solution)/shard_map/ppermute | solution.py:58
  17.9 32.7 %collective-permute-start.4 = (bf16[256,2048]{0,1:T(8,128)(2,1)}, bf16[256,2048]{0,1:T(8,128)(2,1)}, u32[]{:S(2)}, u32[]{:S(2)}) collective-permute-start(bf16[256,2048]{0,1:T(8,128)(2,1)} %pad_maximum_fusion), channel_id=1, source_target_pairs={{0,64},{64,0},{1,65},{65,1},{2,66},{66,2},{3,67},{67,3},{4,68},{68... | collective-permute-start | bytes 3145736 | tf_op jit(solution)/shard_map/ppermute | solution.py:44
  37.9 56.5 %collective-permute-start.3 = (bf16[256,2048]{0,1:T(8,128)(2,1)}, bf16[256,2048]{0,1:T(8,128)(2,1)}, u32[]{:S(2)}, u32[]{:S(2)}) collective-permute-start(bf16[256,2048]{0,1:T(8,128)(2,1)} %broadcast_select_fusion.3), channel_id=1, source_target_pairs={{0,16},{16,32},{32,48},{48,0},{8,56},{24,8},{40,24},{56,40},{1,17}... | collective-permute-start | bytes 3145736 | tf_op jit(solution)/shard_map/ppermute | solution.py:62
  50.5 28.5 %collective-permute-start.5 = (bf16[256,2048]{0,1:T(8,128)(2,1)}, bf16[256,2048]{0,1:T(8,128)(2,1)S(1)}, u32[]{:S(2)}, u32[]{:S(2)}) collective-permute-start(bf16[256,2048]{0,1:T(8,128)(2,1)} %collective-permute-done.4), channel_id=1, source_target_pairs={{0,16},{16,32},{32,48},{48,0},{1,17},{17,33},{33,49},{49,1},{2,18}... | collective-permute-start | bytes 3145736 | tf_op jit(solution)/shard_map/ppermute | solution.py:57
  52.6 26.4 %collective-permute-start.6 = (bf16[256,2048]{0,1:T(8,128)(2,1)}, bf16[256,2048]{0,1:T(8,128)(2,1)S(1)}, u32[]{:S(2)}, u32[]{:S(2)}) collective-permute-start(bf16[256,2048]{0,1:T(8,128)(2,1)} %collective-permute-done.4), channel_id=1, source_target_pairs={{0,48},{16,0},{32,16},{48,32},{1,49},{17,1},{33,17},{49,33},{2,50}... | collective-permute-start | bytes 3145736 | tf_op jit(solution)/shard_map/ppermute | solution.py:58
  58.0 23.1 %copy-start.9 = (bf16[2048,1536]{0,1:T(8,128)(2,1)}, bf16[2048,1536]{0,1:T(8,128)(2,1)S(1)}, u32[]{:S(2)}) copy-start(bf16[2048,1536]{0,1:T(8,128)(2,1)S(1)} %slice_dynamic-update-slice_fusion.5) | copy-start | bytes 18874372
  79.0 2.1 copy-start.5
  79.0 1.0 copy-start.3
  80.0 7.0 %copy-start.11 = (f32[1,4096]{1,0:T(1,128)S(1)}, f32[1,4096]{1,0:T(1,128)}, u32[]{:S(2)}) copy-start(f32[1,4096]{1,0:T(1,128)} %param.12) | copy-start | bytes 49156
  80.0 7.0 %copy-start.12 = (f32[1,4096]{1,0:T(1,128)S(1)}, f32[1,4096]{1,0:T(1,128)}, u32[]{:S(2)}) copy-start(f32[1,4096]{1,0:T(1,128)} %param.13) | copy-start | bytes 49156
  81.1 16.1 %collective-permute-start.7 = (bf16[256,2048]{0,1:T(8,128)(2,1)}, bf16[256,2048]{0,1:T(8,128)(2,1)}, u32[]{:S(2)}, u32[]{:S(2)}) collective-permute-start(bf16[256,2048]{0,1:T(8,128)(2,1)} %broadcast_select_fusion.2), channel_id=1, source_target_pairs={{0,16},{16,32},{32,48},{48,0},{8,56},{24,8},{40,24},{56,40},{1,17}... | collective-permute-start | bytes 3145736 | tf_op jit(solution)/shard_map/ppermute | solution.py:62
  84.1 2.2 copy-start.1
  86.3 8.1 %copy-start.10 = (bf16[2048,1536]{0,1:T(8,128)(2,1)S(1)}, bf16[2048,1536]{0,1:T(8,128)(2,1)}, u32[]{:S(2)}) copy-start(bf16[2048,1536]{0,1:T(8,128)(2,1)} %copy-done.9) | copy-start | bytes 18874372
  88.1 8.8 %copy-start.6 = (bf16[256,2048]{0,1:T(8,128)(2,1)S(1)}, bf16[256,2048]{0,1:T(8,128)(2,1)}, u32[]{:S(2)}) copy-start(bf16[256,2048]{0,1:T(8,128)(2,1)} %copy-done.5) | copy-start | bytes 3145732
  88.1 8.9 %copy-start.4 = (bf16[256,2048]{0,1:T(8,128)(2,1)S(1)}, bf16[256,2048]{0,1:T(8,128)(2,1)}, u32[]{:S(2)}) copy-start(bf16[256,2048]{0,1:T(8,128)(2,1)} %copy-done.3) | copy-start | bytes 3145732
  88.1 10.4 %collective-permute-start = (bf16[256,4096]{1,0:T(8,128)(2,1)S(1)}, bf16[256,4096]{1,0:T(8,128)(2,1)S(1)}, u32[]{:S(2)}, u32[]{:S(2)}) collective-permute-start(bf16[256,4096]{1,0:T(8,128)(2,1)S(1)} %fusion.30), channel_id=1, source_target_pairs={{0,8},{8,0},{1,9},{9,1},{2,10},{10,2},{3,11},{11,3},{4,12},{12,4},... | collective-permute-start | bytes 6291464 | tf_op jit(solution)/shard_map/ppermute | solution.py:44
  102.5 14.0 %collective-permute-start.8 = (bf16[256,1536]{1,0:T(8,128)(2,1)S(1)}, bf16[256,1536]{1,0:T(8,128)(2,1)S(1)}, u32[]{:S(2)}, u32[]{:S(2)}) collective-permute-start(bf16[256,1536]{1,0:T(8,128)(2,1)S(1)} %slice.225), channel_id=1, source_target_pairs={{0,8},{8,0},{1,9},{9,1},{2,10},{10,2},{3,11},{11,3},{4,12},{12,4},... | collective-permute-start | bytes 2359304 | tf_op jit(solution)/shard_map/ppermute | solution.py:44
  114.0 2.7 %copy-start.13 = (s32[1,16]{1,0:T(1,128)S(1)}, s32[1,16]{1,0:T(1,128)}, u32[]{:S(2)}) copy-start(s32[1,16]{1,0:T(1,128)} %param.15) | copy-start | bytes 196
  120.5 4.4 %collective-permute-start.9 = (bf16[256,512]{0,1:T(8,128)(2,1)S(1)}, bf16[256,512]{0,1:T(8,128)(2,1)S(1)}, u32[]{:S(2)}, u32[]{:S(2)}) collective-permute-start(bf16[256,512]{0,1:T(8,128)(2,1)S(1)} %get-tuple-element.46), channel_id=1, source_target_pairs={{0,8},{8,0},{1,9},{9,1},{2,10},{10,2},{3,11},{11,3},{4,12},{12,4},... | collective-permute-start | bytes 786440 | tf_op jit(solution)/shard_map/ppermute | solution.py:44
  128.3 72.8 %copy-start.7 = (bf16[1,1,256,512]{3,2,1,0:T(8,128)(2,1)S(1)}, bf16[1,1,256,512]{3,2,1,0:T(8,128)(2,1)}, u32[]{:S(2)}) copy-start(bf16[1,1,256,512]{3,2,1,0:T(8,128)(2,1)} %param.9) | copy-start | bytes 786436
  128.5 1.3 copy-start.2
  193.0 8.1 %collective-permute-start.10 = (bf16[256,256]{1,0:T(8,128)(2,1)S(1)}, bf16[256,256]{1,0:T(8,128)(2,1)S(1)}, u32[]{:S(2)}, u32[]{:S(2)}) collective-permute-start(bf16[256,256]{1,0:T(8,128)(2,1)S(1)} %get-tuple-element.45), channel_id=1, source_target_pairs={{0,8},{8,0},{1,9},{9,1},{2,10},{10,2},{3,11},{11,3},{4,12},{12,4},... | collective-permute-start | bytes 393224 | tf_op jit(solution)/shard_map/ppermute | solution.py:44
  202.0 11.1 %all-to-all-start = ((bf16[2,8,16,512]{3,2,0,1:T(8,128)(2,1)}), bf16[2,8,16,512]{3,2,0,1:T(8,128)(2,1)S(1)}, u32[]{:S(2)}, u32[]{:S(2)}) async-start(bf16[2,8,16,512]{3,2,0,1:T(8,128)(2,1)} %copy.43), calls=%async_computation.1 | async-start | bytes 524288 | tf_op jit(solution)/shard_map/all_to_all | solution.py:78
  213.0 9.5 %collective-permute-start.11 = (bf16[8,16,512]{2,1,0:T(8,128)(2,1)S(1)}, bf16[8,16,512]{2,1,0:T(8,128)(2,1)S(1)}, u32[]{:S(2)}, u32[]{:S(2)}) collective-permute-start(bf16[8,16,512]{2,1,0:T(8,128)(2,1)S(1)} %fusion.53), channel_id=1, source_target_pairs={{0,128},{64,192},{128,256},{192,320},{256,384},{320,448},{384,0},{... | collective-permute-start | bytes 393224 | tf_op jit(solution)/shard_map/ppermute | solution.py:82
  216.4 14.7 %collective-permute-start.12 = (bf16[8,16,512]{2,1,0:T(8,128)(2,1)S(1)}, bf16[8,16,512]{2,1,0:T(8,128)(2,1)S(1)}, u32[]{:S(2)}, u32[]{:S(2)}) collective-permute-start(bf16[8,16,512]{2,1,0:T(8,128)(2,1)S(1)} %fusion.52), channel_id=1, source_target_pairs={{0,192},{64,128},{128,320},{192,256},{256,448},{320,384},{384,64},... | collective-permute-start | bytes 393224 | tf_op jit(solution)/shard_map/ppermute | solution.py:87
Sparse Core Ops, SparseCore 0:
  9.4 44.6 all-gather.1
  129.9 62.0 reduce-scatter.1
where the time goes:
time: 240 us; the launch traced here: 239 us
  waiting for transfers between devices  114 us (48%)
  starting transfers between devices  71.2 us (30%)
  local copies, waits for them, and re-layouts  19.7 us (8%)
  between operations  14.1 us (6%)
  other arithmetic  11.3 us (5%)
  matrix products  7.79 us (3%)
    reduce_scatter x1, waiting for transfers between devices, on_device(): pair_sum = lax.psum_scatter(partials, 'mp', scatter_dimension=1, tiled=True)  62.2 us
    ppermute x5, starting transfers between devices, swap(): return lax.ppermute(block, axis, [(0, 1), (1, 0)])  35.2 us
    ppermute x2, waiting for transfers between devices, spread_seq(): ahead = lax.ppermute(piece, 'x', [(k, (k + 1) % nx) for k in range(nx)])  24.6 us
    unnamed x43, local copies, waits for them, and re-layouts  14.1 us
    ppermute x1, waiting for transfers between devices, relay_onward(): lax.ppermute(cross, ('segment', 'zh'), [(to(s, h), to((s + 1) % sections,...  8.52 us
    ppermute x2, starting transfers between devices, spread_seq(): far = lax.ppermute(onward, ('x', 'c'), pairs)  8.34 us
    ppermute x5, waiting for transfers between devices, swap(): return lax.ppermute(block, axis, [(0, 1), (1, 0)])  8.2 us
    ppermute x2, starting transfers between devices, spread_seq(): behind = lax.ppermute(piece, 'x', [(k, (k - 1) % nx) for k in range(nx)])  7.62 us
  transfers between devices with their start and end apart: 16, of which 9 were waited for; matrix products, arithmetic and copies ran while one was open for 9% of the time, Pallas kernels for 0%

commit v1 on v0

--- a/solution.py
+++ b/solution.py
@@ -114,15 +114,18 @@
     arrived = spread_seq(payload)
     core = lax.axis_index("c")
     pair_rows = jnp.concatenate([modulated, swap(modulated, "c")], axis=0)
-    w_in = jnp.concatenate([piece[:, :columns] for _, piece in arrived], axis=0)
-    reordered = jnp.concatenate(
-        [
-            lax.dynamic_slice_in_dim(pair_rows, (chip * 2 + core) * rows, rows, axis=1)
-            for chip, _ in arrived
-        ],
-        axis=1,
-    )
-    both = jnp.dot(reordered, w_in, preferred_element_type=jnp.float32)
+    both = None
+    for group in (arrived[:4], arrived[4:]):
+        w_in = jnp.concatenate([piece[:, :columns] for _, piece in group], axis=0)
+        reordered = jnp.concatenate(
+            [
+                lax.dynamic_slice_in_dim(pair_rows, (chip * 2 + core) * rows, rows, axis=1)
+                for chip, _ in group
+            ],
+            axis=1,
+        )
+        part = jnp.dot(reordered, w_in, preferred_element_type=jnp.float32)
+        both = part if both is None else both + part
     projected = both[:patches] + swap(both[patches:].astype(jnp.bfloat16), "c").astype(
         jnp.float32
     )

time: 240 us -> 239 us (level)
  starting transfers between devices: 71.2 us -> 65.9 us
  other arithmetic: 11.3 us -> 14.9 us
    ppermute x2, waiting for transfers between devices: 24.6 us -> 0.79 us  [spread_seq(): ahead = lax.ppermute(piece, 'x', [(k, (k + 1) % nx) for k in range(nx)])]
    ppermute x2, waiting for transfers between devices: 0.14 us -> 12.1 us  [spread_seq(): far = lax.ppermute(onward, ('x', 'c'), pairs)]
    ppermute x5, waiting for transfers between devices: 8.2 us -> 16.8 us  [swap(): return lax.ppermute(block, axis, [(0, 1), (1, 0)])]
    slice x0 -> x8, local copies, waits for them, and re-layouts: none -> 7.14 us  [on_device(): w_in = jnp.concatenate([piece[:, :columns] for _, piece in group], axis=0)]
    ppermute x5, starting transfers between devices: 35.2 us -> 29.6 us  [swap(): return lax.ppermute(block, axis, [(0, 1), (1, 0)])]
    unnamed x43 -> x34, local copies, waits for them, and re-layouts: 14.1 us -> 9.58 us
    concatenate x1 -> x2, other arithmetic: 0.04 us -> 2.47 us  [on_device(): pair_rows = jnp.concatenate([modulated, swap(modulated, 'c')], axis=0)]
  transfers between devices with their start and end apart: 16 -> 16, of which waited for: 9 -> 10; matrix products, arithmetic and copies ran while one was open for 9% -> 11% of each run, Pallas kernels for 0% -> 0%
where the time goes in v1:
time: 239 us; the launch traced here: 237 us
  waiting for transfers between devices  113 us (47%)
  starting transfers between devices  65.9 us (28%)
  local copies, waits for them, and re-layouts  21.1 us (9%)
  other arithmetic  14.9 us (6%)
  between operations  14.1 us (6%)
  matrix products  7.98 us (3%)
    reduce_scatter x1, waiting for transfers between devices, on_device(): pair_sum = lax.psum_scatter(partials, 'mp', scatter_dimension=1, tiled=True)  63.8 us
    ppermute x5, starting transfers between devices, swap(): return lax.ppermute(block, axis, [(0, 1), (1, 0)])  29.6 us
    ppermute x5, waiting for transfers between devices, swap(): return lax.ppermute(block, axis, [(0, 1), (1, 0)])  16.8 us
    ppermute x2, waiting for transfers between devices, spread_seq(): far = lax.ppermute(onward, ('x', 'c'), pairs)  12.1 us
    unnamed x34, local copies, waits for them, and re-layouts  9.58 us
    ppermute x2, starting transfers between devices, spread_seq(): far = lax.ppermute(onward, ('x', 'c'), pairs)  8.54 us
    ppermute x1, waiting for transfers between devices, relay_onward(): lax.ppermute(cross, ('segment', 'zh'), [(to(s, h), to((s + 1) % sections,...  8.52 us
    ppermute x2, starting transfers between devices, spread_seq(): ahead = lax.ppermute(piece, 'x', [(k, (k + 1) % nx) for k in range(nx)])  7.16 us
  transfers between devices with their start and end apart: 16, of which 10 were waited for; matrix products, arithmetic and copies ran while one was open for 11% of the time, Pallas kernels for 0%

profile of v1, /device:TPU:1, one launch (start us, length us, event | category | flops | bytes accessed | tf_op | source)
XLA Modules:
  0.0 237.4 jit_solution(7570883811440709859)
XLA Ops:
  7.3 1.4 copy.41
  8.7 2.2 pad_maximum_fusion
  10.9 11.4 %collective-permute-start.4 = (bf16[256,2048]{0,1:T(8,128)(2,1)}, bf16[256,2048]{0,1:T(8,128)(2,1)}, u32[]{:S(2)}, u32[]{:S(2)}) collective-permute-start(bf16[256,2048]{0,1:T(8,128)(2,1)} %pad_maximum_fusion), channel_id=1, source_target_pairs={{0,64},{64,0},{1,65},{65,1},{2,66},{66,2},{3,67},{67,3},{4,68},{68... | collective-permute-start | bytes 3145736 | tf_op jit(solution)/shard_map/ppermute | solution.py:44
  22.4 3.1 %collective-permute-start.1 = (bf16[256,2048]{0,1:T(8,128)(2,1)}, bf16[256,2048]{0,1:T(8,128)(2,1)}, u32[]{:S(2)}, u32[]{:S(2)}) collective-permute-start(bf16[256,2048]{0,1:T(8,128)(2,1)} %pad_maximum_fusion), channel_id=1, source_target_pairs={{0,16},{16,32},{32,48},{48,0},{1,17},{17,33},{33,49},{49,1},{2,18}... | collective-permute-start | bytes 3145736 | tf_op jit(solution)/shard_map/ppermute | solution.py:57
  25.5 3.4 %collective-permute-start.2 = (bf16[256,2048]{0,1:T(8,128)(2,1)}, bf16[256,2048]{0,1:T(8,128)(2,1)}, u32[]{:S(2)}, u32[]{:S(2)}) collective-permute-start(bf16[256,2048]{0,1:T(8,128)(2,1)} %pad_maximum_fusion), channel_id=1, source_target_pairs={{0,48},{16,0},{32,16},{48,32},{1,49},{17,1},{33,17},{49,33},{2,50}... | collective-permute-start | bytes 3145736 | tf_op jit(solution)/shard_map/ppermute | solution.py:58
  28.9 15.9 %collective-permute-done.4 = bf16[256,2048]{0,1:T(8,128)(2,1)} collective-permute-done((bf16[256,2048]{0,1:T(8,128)(2,1)}, bf16[256,2048]{0,1:T(8,128)(2,1)}, u32[]{:S(2)}, u32[]{:S(2)}) %collective-permute-start.4) | collective-permute-done | bytes 1048608 | tf_op jit(solution)/shard_map/ppermute | solution.py:44
  44.8 4.0 %collective-permute-start.5 = (bf16[256,2048]{0,1:T(8,128)(2,1)}, bf16[256,2048]{0,1:T(8,128)(2,1)}, u32[]{:S(2)}, u32[]{:S(2)}) collective-permute-start(bf16[256,2048]{0,1:T(8,128)(2,1)} %collective-permute-done.4), channel_id=1, source_target_pairs={{0,16},{16,32},{32,48},{48,0},{1,17},{17,33},{33,49},{49,1},{2,18}... | collective-permute-start | bytes 3145736 | tf_op jit(solution)/shard_map/ppermute | solution.py:57
  48.8 3.2 %collective-permute-start.6 = (bf16[256,2048]{0,1:T(8,128)(2,1)}, bf16[256,2048]{0,1:T(8,128)(2,1)S(1)}, u32[]{:S(2)}, u32[]{:S(2)}) collective-permute-start(bf16[256,2048]{0,1:T(8,128)(2,1)} %collective-permute-done.4), channel_id=1, source_target_pairs={{0,48},{16,0},{32,16},{48,32},{1,49},{17,1},{33,17},{49,33},{2,50}... | collective-permute-start | bytes 3145736 | tf_op jit(solution)/shard_map/ppermute | solution.py:58
  52.0 2.1 all-gather.2.cloned.1.call-done
  54.1 2.1 convert_reduce_fusion
  57.1 1.0 fusion.30
  58.1 6.5 %collective-permute-start = (bf16[256,4096]{1,0:T(8,128)(2,1)S(1)}, bf16[256,4096]{1,0:T(8,128)(2,1)}, u32[]{:S(2)}, u32[]{:S(2)}) collective-permute-start(bf16[256,4096]{1,0:T(8,128)(2,1)S(1)} %fusion.30), channel_id=1, source_target_pairs={{0,8},{8,0},{1,9},{9,1},{2,10},{10,2},{3,11},{11,3},{4,12},{12,4},... | collective-permute-start | bytes 6291464 | tf_op jit(solution)/shard_map/ppermute | solution.py:44
  64.6 2.3 broadcast_select_fusion.3
  66.9 4.4 %collective-permute-start.3 = (bf16[256,2048]{0,1:T(8,128)(2,1)}, bf16[256,2048]{0,1:T(8,128)(2,1)}, u32[]{:S(2)}, u32[]{:S(2)}) collective-permute-start(bf16[256,2048]{0,1:T(8,128)(2,1)} %broadcast_select_fusion.3), channel_id=1, source_target_pairs={{0,16},{16,32},{32,48},{48,0},{8,56},{24,8},{40,24},{56,40},{1,17}... | collective-permute-start | bytes 3145736 | tf_op jit(solution)/shard_map/ppermute | solution.py:62
  72.2 2.0 collective-permute-done.6
  74.2 1.2 broadcast_select_fusion.2
  75.4 4.1 %collective-permute-start.7 = (bf16[256,2048]{0,1:T(8,128)(2,1)}, bf16[256,2048]{0,1:T(8,128)(2,1)}, u32[]{:S(2)}, u32[]{:S(2)}) collective-permute-start(bf16[256,2048]{0,1:T(8,128)(2,1)} %broadcast_select_fusion.2), channel_id=1, source_target_pairs={{0,16},{16,32},{32,48},{48,0},{8,56},{24,8},{40,24},{56,40},{1,17}... | collective-permute-start | bytes 3145736 | tf_op jit(solution)/shard_map/ppermute | solution.py:62
  79.7 1.2 slice.142
  80.9 1.2 slice.139
  82.0 1.2 slice.140
  83.2 1.0 slice_dynamic-update-slice_fusion.14
  84.2 1.2 slice.143
  85.4 1.7 collective-permute-done.3
  87.2 1.2 slice.141
  88.3 10.3 %collective-permute-done.7 = bf16[256,2048]{0,1:T(8,128)(2,1)} collective-permute-done((bf16[256,2048]{0,1:T(8,128)(2,1)}, bf16[256,2048]{0,1:T(8,128)(2,1)}, u32[]{:S(2)}, u32[]{:S(2)}) %collective-permute-start.7) | collective-permute-done | bytes 1048608 | tf_op jit(solution)/shard_map/ppermute | solution.py:62
  98.7 1.2 slice.145
  99.9 1.0 fusion.72
  100.9 1.4 fusion.66
  102.4 1.8 fusion.38
  104.2 1.8 convolution_add_fusion
  106.2 2.7 %collective-permute-start.8 = (bf16[256,1536]{1,0:T(8,128)(2,1)S(1)}, bf16[256,1536]{1,0:T(8,128)(2,1)S(1)}, u32[]{:S(2)}, u32[]{:S(2)}) collective-permute-start(bf16[256,1536]{1,0:T(8,128)(2,1)S(1)} %slice.218), channel_id=1, source_target_pairs={{0,8},{8,0},{1,9},{9,1},{2,10},{10,2},{3,11},{11,3},{4,12},{12,4},... | collective-permute-start | bytes 2359304 | tf_op jit(solution)/shard_map/ppermute | solution.py:44
  109.8 1.0 slice_dynamic-update-slice_fusion.12
  110.8 1.0 slice_dynamic-update-slice_fusion.11
  111.8 1.0 slice_dynamic-update-slice_fusion.10
  113.1 1.1 copy-done.9
  114.1 3.6 %conditional.1 = (bf16[256,512]{0,1:T(8,128)(2,1)S(1)}) conditional(s32[]{:T(128)} %convert_element_type.58, (s32[]{:T(128)}, s32[1,16]{1,0:T(1,128)S(1)}, bf16[256,1536]{1,0:T(8,128)(2,1)S(1)}) %tuple.31, (s32[]{:T(128)}, s32[16]{0:T(128)S(1)}, s32[1,16]{1,0:T(1,128)S(1)}, bf16[256,1536]{1,0:T(8,128)(2,1)S(1)}) %tuple.32), branch_computations={%region_2.5_spmd, %region_5.9_spmd} | conditional | flops 204410160 | bytes 6552408 | solution.py:150
  117.7 1.9 collective-permute-start.9
  120.4 1.7 slice_dynamic-update-slice_fusion.8
  122.1 2.9 %convolution_convert_fusion.2 = bf16[512,2048]{1,0:T(8,128)(2,1)S(1)} fusion(bf16[2048,512]{0,1:T(8,128)(2,1)} %slice_dynamic-update-slice_fusion.8, bf16[256,512]{0,1:T(8,128)(2,1)S(1)} %collective-permute-done.9, bf16[256,512]{0,1:T(8,128)(2,1)S(1)} %get-tuple-element.54), kind=kOutput, calls=%fused_computation.87 | convolution fusion | flops 1075838976 | bytes 4718592 | tf_op jit(solution)/shard_map/tr,cr->tc/dot_general | solution.py:156
  125.7 1.3 copy-done.2
  127.0 63.8 %reduce-scatter.2.cloned.1.call-done = bf16[512,256]{1,0:T(8,128)(2,1)} async-done(((bf16[512,2048]{1,0:T(8,128)(2,1)}), bf16[512,256]{1,0:T(8,128)(2,1)}) %reduce-scatter.2.cloned.1.call-update) | async-done | bytes 262160 | tf_op jit(solution)/shard_map/reduce_scatter | solution.py:164
  190.8 1.0 fusion.80
  191.8 7.1 %collective-permute-start.10 = (bf16[256,256]{1,0:T(8,128)(2,1)S(1)}, bf16[256,256]{1,0:T(8,128)(2,1)S(1)}, u32[]{:S(2)}, u32[]{:S(2)}) collective-permute-start(bf16[256,256]{1,0:T(8,128)(2,1)S(1)} %get-tuple-element.53), channel_id=1, source_target_pairs={{0,8},{8,0},{1,9},{9,1},{2,10},{10,2},{3,11},{11,3},{4,12},{12,4},... | collective-permute-start | bytes 393224 | tf_op jit(solution)/shard_map/ppermute | solution.py:44
  200.7 4.7 %all-to-all-start = ((bf16[2,8,16,512]{3,2,0,1:T(8,128)(2,1)}), bf16[2,8,16,512]{3,2,0,1:T(8,128)(2,1)S(1)}, u32[]{:S(2)}, u32[]{:S(2)}) async-start(bf16[2,8,16,512]{3,2,0,1:T(8,128)(2,1)} %copy.43), calls=%async_computation.1 | async-start | bytes 524288 | tf_op jit(solution)/shard_map/all_to_all | solution.py:78
  205.4 6.5 %all-to-all-done = bf16[2,8,16,512]{3,2,0,1:T(8,128)(2,1)S(1)} async-done(((bf16[2,8,16,512]{3,2,0,1:T(8,128)(2,1)}), bf16[2,8,16,512]{3,2,0,1:T(8,128)(2,1)S(1)}, u32[]{:S(2)}, u32[]{:S(2)}) %all-to-all-start) | async-done | bytes 262176 | tf_op jit(solution)/shard_map/all_to_all | solution.py:78
  211.9 3.3 %collective-permute-start.11 = (bf16[8,16,512]{2,1,0:T(8,128)(2,1)S(1)}, bf16[8,16,512]{2,1,0:T(8,128)(2,1)S(1)}, u32[]{:S(2)}, u32[]{:S(2)}) collective-permute-start(bf16[8,16,512]{2,1,0:T(8,128)(2,1)S(1)} %fusion.74), channel_id=1, source_target_pairs={{0,128},{64,192},{128,256},{192,320},{256,384},{320,448},{384,0},{... | collective-permute-start | bytes 393224 | tf_op jit(solution)/shard_map/ppermute | solution.py:82
  215.2 6.1 %collective-permute-start.12 = (bf16[8,16,512]{2,1,0:T(8,128)(2,1)S(1)}, bf16[8,16,512]{2,1,0:T(8,128)(2,1)S(1)}, u32[]{:S(2)}, u32[]{:S(2)}) collective-permute-start(bf16[8,16,512]{2,1,0:T(8,128)(2,1)S(1)} %fusion.73), channel_id=1, source_target_pairs={{0,192},{64,128},{128,320},{192,256},{256,448},{320,384},{384,64},... | collective-permute-start | bytes 393224 | tf_op jit(solution)/shard_map/ppermute | solution.py:87
  221.3 8.5 %collective-permute-done.12 = bf16[8,16,512]{2,1,0:T(8,128)(2,1)S(1)} collective-permute-done((bf16[8,16,512]{2,1,0:T(8,128)(2,1)S(1)}, bf16[8,16,512]{2,1,0:T(8,128)(2,1)S(1)}, u32[]{:S(2)}, u32[]{:S(2)}) %collective-permute-start.12) | collective-permute-done | bytes 131104 | tf_op jit(solution)/shard_map/ppermute | solution.py:87
  (70 shorter events, 11.2 us)
Async XLA Ops:
  6.5 192.4 %copy-start = (f32[1,4096]{1,0:T(1,128)S(1)}, f32[1,4096]{1,0:T(1,128)}, u32[]{:S(2)}) copy-start(f32[1,4096]{1,0:T(1,128)} %param.14) | copy-start | bytes 49156
  6.5 47.6 %all-gather.2.cloned.1.call-start = ((), (), s32[]{:S(2)}) async-start(), calls=%async_computation.2 | async-start | bytes 2359296 | tf_op jit(solution)/shard_map/all_gather | solution.py:103
  7.3 183.6 %reduce-scatter.2.cloned.1.call-start = ((), (), s32[]{:S(2)}) async-start(), calls=%async_computation.3 | async-start | bytes 2359296 | tf_op jit(solution)/shard_map/reduce_scatter | solution.py:164
  8.7 47.5 %copy-start.5 = (bf16[1,256,3,512]{1,3,2,0:T(8,128)(2,1)}, bf16[1,256,3,512]{1,3,2,0:T(8,128)(2,1)S(1)}, u32[]{:S(2)}) copy-start(bf16[1,256,3,512]{1,3,2,0:T(8,128)(2,1)S(1)} %copy.41) | copy-start | bytes 2359300
  10.9 33.9 %collective-permute-start.4 = (bf16[256,2048]{0,1:T(8,128)(2,1)}, bf16[256,2048]{0,1:T(8,128)(2,1)}, u32[]{:S(2)}, u32[]{:S(2)}) collective-permute-start(bf16[256,2048]{0,1:T(8,128)(2,1)} %pad_maximum_fusion), channel_id=1, source_target_pairs={{0,64},{64,0},{1,65},{65,1},{2,66},{66,2},{3,67},{67,3},{4,68},{68... | collective-permute-start | bytes 3145736 | tf_op jit(solution)/shard_map/ppermute | solution.py:44
  22.4 42.2 %collective-permute-start.1 = (bf16[256,2048]{0,1:T(8,128)(2,1)}, bf16[256,2048]{0,1:T(8,128)(2,1)}, u32[]{:S(2)}, u32[]{:S(2)}) collective-permute-start(bf16[256,2048]{0,1:T(8,128)(2,1)} %pad_maximum_fusion), channel_id=1, source_target_pairs={{0,16},{16,32},{32,48},{48,0},{1,17},{17,33},{33,49},{49,1},{2,18}... | collective-permute-start | bytes 3145736 | tf_op jit(solution)/shard_map/ppermute | solution.py:57
  25.5 39.1 %collective-permute-start.2 = (bf16[256,2048]{0,1:T(8,128)(2,1)}, bf16[256,2048]{0,1:T(8,128)(2,1)}, u32[]{:S(2)}, u32[]{:S(2)}) collective-permute-start(bf16[256,2048]{0,1:T(8,128)(2,1)} %pad_maximum_fusion), channel_id=1, source_target_pairs={{0,48},{16,0},{32,16},{48,32},{1,49},{17,1},{33,17},{49,33},{2,50}... | collective-permute-start | bytes 3145736 | tf_op jit(solution)/shard_map/ppermute | solution.py:58
  44.8 27.4 %collective-permute-start.5 = (bf16[256,2048]{0,1:T(8,128)(2,1)}, bf16[256,2048]{0,1:T(8,128)(2,1)}, u32[]{:S(2)}, u32[]{:S(2)}) collective-permute-start(bf16[256,2048]{0,1:T(8,128)(2,1)} %collective-permute-done.4), channel_id=1, source_target_pairs={{0,16},{16,32},{32,48},{48,0},{1,17},{17,33},{33,49},{49,1},{2,18}... | collective-permute-start | bytes 3145736 | tf_op jit(solution)/shard_map/ppermute | solution.py:57
  48.8 25.4 %collective-permute-start.6 = (bf16[256,2048]{0,1:T(8,128)(2,1)}, bf16[256,2048]{0,1:T(8,128)(2,1)S(1)}, u32[]{:S(2)}, u32[]{:S(2)}) collective-permute-start(bf16[256,2048]{0,1:T(8,128)(2,1)} %collective-permute-done.4), channel_id=1, source_target_pairs={{0,48},{16,0},{32,16},{48,32},{1,49},{17,1},{33,17},{49,33},{2,50}... | collective-permute-start | bytes 3145736 | tf_op jit(solution)/shard_map/ppermute | solution.py:58
  54.1 2.2 copy-start.1
  54.1 2.9 %copy-start.10 = (f32[1,4096]{1,0:T(1,128)S(1)}, f32[1,4096]{1,0:T(1,128)}, u32[]{:S(2)}) copy-start(f32[1,4096]{1,0:T(1,128)} %param.12) | copy-start | bytes 49156
  54.1 2.9 %copy-start.11 = (f32[1,4096]{1,0:T(1,128)S(1)}, f32[1,4096]{1,0:T(1,128)}, u32[]{:S(2)}) copy-start(f32[1,4096]{1,0:T(1,128)} %param.13) | copy-start | bytes 49156
  58.1 41.8 %collective-permute-start = (bf16[256,4096]{1,0:T(8,128)(2,1)S(1)}, bf16[256,4096]{1,0:T(8,128)(2,1)}, u32[]{:S(2)}, u32[]{:S(2)}) collective-permute-start(bf16[256,4096]{1,0:T(8,128)(2,1)S(1)} %fusion.30), channel_id=1, source_target_pairs={{0,8},{8,0},{1,9},{9,1},{2,10},{10,2},{3,11},{11,3},{4,12},{12,4},... | collective-permute-start | bytes 6291464 | tf_op jit(solution)/shard_map/ppermute | solution.py:44
  66.9 12.7 %copy-start.8 = (bf16[1,512,256]{2,1,0:T(8,128)(2,1)S(1)}, bf16[1,512,256]{2,1,0:T(8,128)(2,1)}, u32[]{:S(2)}) copy-start(bf16[1,512,256]{2,1,0:T(8,128)(2,1)} %param.11) | copy-start | bytes 786436
  66.9 20.2 %collective-permute-start.3 = (bf16[256,2048]{0,1:T(8,128)(2,1)}, bf16[256,2048]{0,1:T(8,128)(2,1)}, u32[]{:S(2)}, u32[]{:S(2)}) collective-permute-start(bf16[256,2048]{0,1:T(8,128)(2,1)} %broadcast_select_fusion.3), channel_id=1, source_target_pairs={{0,16},{16,32},{32,48},{48,0},{8,56},{24,8},{40,24},{56,40},{1,17}... | collective-permute-start | bytes 3145736 | tf_op jit(solution)/shard_map/ppermute | solution.py:62
  74.2 11.2 %copy-start.3 = (bf16[256,2048]{0,1:T(8,128)(2,1)}, bf16[256,2048]{0,1:T(8,128)(2,1)S(1)}, u32[]{:S(2)}) copy-start(bf16[256,2048]{0,1:T(8,128)(2,1)S(1)} %collective-permute-done.6) | copy-start | bytes 3145732
  75.4 23.3 %collective-permute-start.7 = (bf16[256,2048]{0,1:T(8,128)(2,1)}, bf16[256,2048]{0,1:T(8,128)(2,1)}, u32[]{:S(2)}, u32[]{:S(2)}) collective-permute-start(bf16[256,2048]{0,1:T(8,128)(2,1)} %broadcast_select_fusion.2), channel_id=1, source_target_pairs={{0,16},{16,32},{32,48},{48,0},{8,56},{24,8},{40,24},{56,40},{1,17}... | collective-permute-start | bytes 3145736 | tf_op jit(solution)/shard_map/ppermute | solution.py:62
  100.9 1.5 slice-start
  102.4 1.8 copy-start.6
  106.2 6.6 %collective-permute-start.8 = (bf16[256,1536]{1,0:T(8,128)(2,1)S(1)}, bf16[256,1536]{1,0:T(8,128)(2,1)S(1)}, u32[]{:S(2)}, u32[]{:S(2)}) collective-permute-start(bf16[256,1536]{1,0:T(8,128)(2,1)S(1)} %slice.218), channel_id=1, source_target_pairs={{0,8},{8,0},{1,9},{9,1},{2,10},{10,2},{3,11},{11,3},{4,12},{12,4},... | collective-permute-start | bytes 2359304 | tf_op jit(solution)/shard_map/ppermute | solution.py:44
  110.8 2.2 copy-start.12
  112.8 1.3 copy-start.9
  113.1 6.6 %copy-start.4 = (bf16[256,2048]{0,1:T(8,128)(2,1)S(1)}, bf16[256,2048]{0,1:T(8,128)(2,1)}, u32[]{:S(2)}) copy-start(bf16[256,2048]{0,1:T(8,128)(2,1)} %copy-done.3) | copy-start | bytes 3145732
  117.7 4.4 %collective-permute-start.9 = (bf16[256,512]{0,1:T(8,128)(2,1)S(1)}, bf16[256,512]{0,1:T(8,128)(2,1)S(1)}, u32[]{:S(2)}, u32[]{:S(2)}) collective-permute-start(bf16[256,512]{0,1:T(8,128)(2,1)S(1)} %get-tuple-element.54), channel_id=1, source_target_pairs={{0,8},{8,0},{1,9},{9,1},{2,10},{10,2},{3,11},{11,3},{4,12},{12,4},... | collective-permute-start | bytes 786440 | tf_op jit(solution)/shard_map/ppermute | solution.py:44
  125.5 74.4 %copy-start.7 = (bf16[1,1,256,512]{3,2,1,0:T(8,128)(2,1)S(1)}, bf16[1,1,256,512]{3,2,1,0:T(8,128)(2,1)}, u32[]{:S(2)}) copy-start(bf16[1,1,256,512]{3,2,1,0:T(8,128)(2,1)} %param.9) | copy-start | bytes 786436
  125.6 1.3 copy-start.2
  191.8 8.1 %collective-permute-start.10 = (bf16[256,256]{1,0:T(8,128)(2,1)S(1)}, bf16[256,256]{1,0:T(8,128)(2,1)S(1)}, u32[]{:S(2)}, u32[]{:S(2)}) collective-permute-start(bf16[256,256]{1,0:T(8,128)(2,1)S(1)} %get-tuple-element.53), channel_id=1, source_target_pairs={{0,8},{8,0},{1,9},{9,1},{2,10},{10,2},{3,11},{11,3},{4,12},{12,4},... | collective-permute-start | bytes 393224 | tf_op jit(solution)/shard_map/ppermute | solution.py:44
  200.7 11.1 %all-to-all-start = ((bf16[2,8,16,512]{3,2,0,1:T(8,128)(2,1)}), bf16[2,8,16,512]{3,2,0,1:T(8,128)(2,1)S(1)}, u32[]{:S(2)}, u32[]{:S(2)}) async-start(bf16[2,8,16,512]{3,2,0,1:T(8,128)(2,1)} %copy.43), calls=%async_computation.1 | async-start | bytes 524288 | tf_op jit(solution)/shard_map/all_to_all | solution.py:78
  211.9 9.4 %collective-permute-start.11 = (bf16[8,16,512]{2,1,0:T(8,128)(2,1)S(1)}, bf16[8,16,512]{2,1,0:T(8,128)(2,1)S(1)}, u32[]{:S(2)}, u32[]{:S(2)}) collective-permute-start(bf16[8,16,512]{2,1,0:T(8,128)(2,1)S(1)} %fusion.74), channel_id=1, source_target_pairs={{0,128},{64,192},{128,256},{192,320},{256,384},{320,448},{384,0},{... | collective-permute-start | bytes 393224 | tf_op jit(solution)/shard_map/ppermute | solution.py:82
  215.2 14.7 %collective-permute-start.12 = (bf16[8,16,512]{2,1,0:T(8,128)(2,1)S(1)}, bf16[8,16,512]{2,1,0:T(8,128)(2,1)S(1)}, u32[]{:S(2)}, u32[]{:S(2)}) collective-permute-start(bf16[8,16,512]{2,1,0:T(8,128)(2,1)S(1)} %fusion.73), channel_id=1, source_target_pairs={{0,192},{64,128},{128,320},{192,256},{256,448},{320,384},{384,64},... | collective-permute-start | bytes 393224 | tf_op jit(solution)/shard_map/ppermute | solution.py:87
Sparse Core Ops, SparseCore 0:
  9.4 44.6 all-gather.1
  127.1 63.6 reduce-scatter.1
